TPU v7x, 512 devices: a whole 4x4x16 slice. The times are simulated.
512 devices in a mesh: bond: 32 (over z, core), row: 16 (over y, x).
Axes of the slice: x: 4, y: 4, z: 16, core: 2. Of those that a mesh axis runs over, the one named last changes fastest.
Arguments:
- left_core: float32 [32, 384, 2, 384], P('bond', 'row'), may hold values from -1 to 2
- right_core: float32 [32, 384, 2, 384], P('bond', 'row'), may hold values from -1 to 2
- gate_angles: float32 [32, 6], P('bond'), may hold values from -3.140625 to 3.140625
- sketch: float32 [768, 384], P('bond'), may hold values from -0.21875 to 0.21875
Outputs:
- next_pair: float32 [32, 768, 768], P('bond', 'row')
All inputs are finite; a program needn't handle non-finite values.
Results may differ from a plain program's by a relative error of at most 0.0003.
Values sent between devices are 32-bit elements; how exact they have to be, the bound alone decides.
No kernel may reach another device: no remote copies, remote signals or barrier semaphores. Data moves between devices by JAX's collectives and lax.ppermute only.
A program may use at most 64 MiB of HBM per device.

v0:
```python
import jax
import jax.numpy as jnp
import numpy as np
from jax import lax
from jax.sharding import PartitionSpec as P

ITERS = 2
HIGHEST = lax.Precision.HIGHEST
PLANES = ((0, 1), (2, 3), (0, 2), (1, 3), (0, 3), (1, 2))


def from_behind(value, axis, steps):
    count = lax.axis_size(axis)
    initial, last = (max(0, -steps), min(count, count - steps))
    return lax.ppermute(value, axis, [(source, source + steps) for source in range(initial, last)])


def rotation(first_axis, second_axis, cosine, sine_value):
    unit = np.eye(4, dtype=np.float32)
    diag_part = np.outer(unit[first_axis], unit[first_axis]) + np.outer(
        unit[second_axis], unit[second_axis]
    )
    skew_part = np.outer(unit[second_axis], unit[first_axis]) - np.outer(
        unit[first_axis], unit[second_axis]
    )
    rest_part = np.eye(4, dtype=np.float32) - diag_part
    return (
        jnp.asarray(rest_part)
        + cosine * jnp.asarray(diag_part)
        + sine_value * jnp.asarray(skew_part)
    )


def build_gate(angles):
    gate_matrix = jnp.eye(4, dtype=jnp.float32)
    for number, plane in enumerate(PLANES):
        rotated = rotation(plane[0], plane[1], jnp.cos(angles[number]), jnp.sin(angles[number]))
        gate_matrix = jnp.dot(
            rotated, gate_matrix, precision=HIGHEST, preferred_element_type=jnp.float32
        )
    return gate_matrix


def apply_gate(two_site, gate_matrix):
    width = two_site.shape[1] // 2
    blocks = two_site.reshape(two_site.shape[0] // 2, 2, 2, width)
    mixed_gate = jnp.einsum(
        "pqtu,atuc->apqc", gate_matrix.reshape(2, 2, 2, 2), blocks, precision=HIGHEST
    )
    return mixed_gate.reshape(two_site.shape)


def matmul(left_side, right_side):
    return jnp.dot(left_side, right_side, precision=HIGHEST, preferred_element_type=jnp.float32)


def inner_rows(left_side, right_side):
    return lax.dot_general(
        left_side,
        right_side,
        (((0,), (0,)), ((), ())),
        precision=HIGHEST,
        preferred_element_type=jnp.float32,
    )


def orthonormal(sketched):
    gram_matrix = lax.psum(inner_rows(sketched, sketched), "row")
    chol_factor = jnp.linalg.cholesky(gram_matrix)
    return lax.linalg.triangular_solve(
        chol_factor, sketched, left_side=False, lower=True, transpose_a=True
    )


def on_device(left_core, right_core, gate_angles, sketch):
    width = left_core.shape[3]
    local_sites = left_core.shape[1]
    local_rows = 2 * local_sites
    left_matrix = left_core.reshape(local_rows, width)
    shard_part = lax.all_gather(right_core, "row", axis=1, tiled=True)
    count = shard_part.shape[1]
    two_site = matmul(left_matrix, shard_part.reshape(count, 2 * width))
    two_site = apply_gate(two_site, build_gate(gate_angles[0]))
    shard_part = lax.all_gather(sketch, "bond", axis=0, tiled=True)
    sketched = matmul(two_site, shard_part)
    ortho_basis = orthonormal(sketched)
    for repeat in range(ITERS):
        projected = lax.psum(inner_rows(two_site, ortho_basis), "row")
        ortho_basis = orthonormal(matmul(two_site, projected))
    carried = lax.psum_scatter(
        inner_rows(ortho_basis, two_site), "row", scatter_dimension=0, tiled=True
    )
    incoming = from_behind(carried, "bond", 1)
    incoming_matrix = incoming.reshape(local_rows, width)
    stacked_final = ortho_basis.reshape(local_sites, 2, width)
    shard_part = lax.all_gather(stacked_final, "row", axis=0, tiled=True)
    count = shard_part.shape[0]
    next_block = matmul(incoming_matrix, shard_part.reshape(count, 2 * width))
    return next_block[None]


def solution(mesh):
    return jax.shard_map(
        on_device,
        mesh=mesh,
        in_specs=(
            P("bond", "row", None, None),
            P("bond", "row", None, None),
            P("bond", None),
            P("bond", None),
        ),
        out_specs=P("bond", "row", None),
        check_vma=False,
    )
```

profile of v0, /device:TPU:2, one launch (start us, length us, event | category | flops | bytes accessed | tf_op | source)
XLA Modules:
  0.0 1195.2 jit_solution(12344548351591145168)
XLA Ops:
  8.1 1.5 fusion.124
  18.0 0.8 fusion.85
  18.9 0.9 fusion.86
  19.7 0.9 fusion.87
  20.6 0.9 fusion.88
  21.4 0.9 fusion.89
  22.3 0.9 fusion.90
  23.2 49.4 %all-gather.4.cloned.1.call-done = f32[1,384,2,384]{3,2,0,1:T(2,128)} async-done(((f32[1,24,2,384]{3,2,0,1:T(2,128)}), f32[1,384,2,384]{3,2,0,1:T(2,128)}) %all-gather.4.cloned.1.call-update) | async-done | bytes 1179664 | tf_op jit(solution)/shard_map/all_gather | solution.py:80
  72.7 1.3 copy.48
  74.9 0.8 fusion.2
  76.4 68.8 %all-gather.6.cloned.1.call-done = f32[768,384]{1,0:T(8,128)} async-done(((f32[24,384]{1,0:T(8,128)}), f32[768,384]{1,0:T(8,128)}) %all-gather.6.cloned.1.call-update) | async-done | bytes 1179664 | tf_op jit(solution)/shard_map/all_gather | solution.py:84
  145.2 2.0 fusion.125
  147.2 1.5 fusion.126
  149.2 112.5 %all-reduce.8.cloned.1.call-done = f32[384,384]{0,1:T(8,128)} async-done(((f32[384,384]{0,1:T(8,128)}), f32[384,384]{0,1:T(8,128)}) %all-reduce.8.cloned.1.call-update) | async-done | bytes 589840 | tf_op jit(solution)/shard_map/psum | solution.py:68
  261.8 1.4 copy.33
  263.2 11.7 cholesky.273
  275.0 9.8 custom-call.23
  285.4 11.7 cholesky.292
  297.2 9.9 custom-call.24
  307.6 11.7 cholesky.311
  319.4 0.7 compare_reduce_fusion.6
  322.7 6.1 while.6
  323.4 1.3 bitcast_dynamic-update-slice_fusion.6
  325.4 1.3 bitcast_dynamic-update-slice_fusion.6
  327.5 1.3 bitcast_dynamic-update-slice_fusion.6
  328.8 29.5 %custom-call.25 = f32[3,128,128]{1,2,0:T(8,128)S(1)} custom-call(f32[3,128,128]{2,1,0:T(8,128)S(1)} %get-tuple-element.27), custom_call_target="InvertDiagBlocksLowerTriangular" | custom-call | tf_op jit(solution)/shard_map/triangular_solve/custom-call.2 | solution.py:70
  359.4 2.2 fusion.22
  361.6 117.3 %all-reduce.10.cloned.1.call-done = f32[768,384]{1,0:T(8,128)} async-done(((f32[768,384]{1,0:T(8,128)}), f32[768,384]{1,0:T(8,128)}) %all-reduce.10.cloned.1.call-update) | async-done | bytes 1179664 | tf_op jit(solution)/shard_map/psum | solution.py:88
  478.9 2.0 fusion.127
  480.9 1.5 fusion.128
  482.6 115.5 %all-reduce.12.cloned.1.call-done = f32[384,384]{0,1:T(8,128)} async-done(((f32[384,384]{0,1:T(8,128)}), f32[384,384]{0,1:T(8,128)}) %all-reduce.12.cloned.1.call-update) | async-done | bytes 589840 | tf_op jit(solution)/shard_map/psum | solution.py:68
  598.1 1.4 copy.35
  599.6 11.7 cholesky.326
  611.4 9.8 custom-call.26
  621.8 11.7 cholesky.345
  633.5 10.2 custom-call.27
  644.2 11.7 cholesky.364
  659.9 6.1 while.7
  660.6 1.3 bitcast_dynamic-update-slice_fusion.7
  662.6 1.3 bitcast_dynamic-update-slice_fusion.7
  664.7 1.3 bitcast_dynamic-update-slice_fusion.7
  666.0 29.5 %custom-call.28 = f32[3,128,128]{1,2,0:T(8,128)S(1)} custom-call(f32[3,128,128]{2,1,0:T(8,128)S(1)} %get-tuple-element.28), custom_call_target="InvertDiagBlocksLowerTriangular" | custom-call | tf_op jit(solution)/shard_map/triangular_solve/custom-call.2 | solution.py:70
  696.6 2.2 fusion.28
  698.8 117.3 %all-reduce.14.cloned.1.call-done = f32[768,384]{1,0:T(8,128)} async-done(((f32[768,384]{1,0:T(8,128)}), f32[768,384]{1,0:T(8,128)}) %all-reduce.14.cloned.1.call-update) | async-done | bytes 1179664 | tf_op jit(solution)/shard_map/psum | solution.py:88
  816.1 2.0 fusion.129
  818.1 1.5 fusion.130
  819.8 115.5 %all-reduce.16.cloned.1.call-done = f32[384,384]{0,1:T(8,128)} async-done(((f32[384,384]{0,1:T(8,128)}), f32[384,384]{0,1:T(8,128)}) %all-reduce.16.cloned.1.call-update) | async-done | bytes 589840 | tf_op jit(solution)/shard_map/psum | solution.py:68
  935.3 1.4 copy.37
  936.8 11.7 cholesky.379
  948.6 9.8 custom-call.29
  959.0 11.7 cholesky.398
  970.7 10.0 custom-call.30
  981.2 11.7 cholesky.417
  996.9 6.1 while.8
  997.6 1.3 bitcast_dynamic-update-slice_fusion.8
  999.6 1.3 bitcast_dynamic-update-slice_fusion.8
  1001.7 1.3 bitcast_dynamic-update-slice_fusion.8
  1003.0 29.5 %custom-call.31 = f32[3,128,128]{1,2,0:T(8,128)S(1)} custom-call(f32[3,128,128]{2,1,0:T(8,128)S(1)} %get-tuple-element.29), custom_call_target="InvertDiagBlocksLowerTriangular" | custom-call | tf_op jit(solution)/shard_map/triangular_solve/custom-call.2 | solution.py:70
  1033.6 2.1 fusion.120
  1036.5 88.4 %reduce-scatter.4.cloned.1.call-done = f32[24,768]{1,0:T(8,128)} async-done(((f32[384,768]{1,0:T(8,128)}), f32[24,768]{1,0:T(8,128)}) %reduce-scatter.4.cloned.1.call-update) | async-done | bytes 73744
  1124.9 1.3 collective-permute-start
  1126.2 59.4 %all-gather.8.cloned.1.call-done = f32[384,2,384]{2,1,0:T(2,128)} async-done(((f32[24,2,384]{2,1,0:T(2,128)}), f32[384,2,384]{2,1,0:T(2,128)}) %all-gather.8.cloned.1.call-update) | async-done | bytes 1179664 | tf_op jit(solution)/shard_map/all_gather | solution.py:96
  1185.5 1.3 copy.50
  1186.9 1.5 convolution_bitcast_fusion
  (115 shorter events, 22.7 us)
Async XLA Ops:
  6.5 66.1 %all-gather.4.cloned.1.call-start = ((), (), s32[]{:S(2)}) async-start(), calls=%async_computation.1 | async-start | bytes 1253376 | tf_op jit(solution)/shard_map/all_gather | solution.py:80
  7.3 138.0 %all-gather.6.cloned.1.call-start = ((), (), s32[]{:S(2)}) async-start(), calls=%async_computation.2 | async-start | bytes 1216512 | tf_op jit(solution)/shard_map/all_gather | solution.py:84
  8.0 253.8 %all-reduce.8.cloned.1.call-start = ((), (), s32[]{:S(2)}) async-start(), calls=%async_computation.3 | async-start | bytes 1179648 | tf_op jit(solution)/shard_map/psum | solution.py:68
  74.0 0.9 copy-start.3
  148.7 330.2 %all-reduce.10.cloned.1.call-start = ((), (), s32[]{:S(2)}) async-start(), calls=%async_computation.4 | async-start | bytes 2359296 | tf_op jit(solution)/shard_map/psum | solution.py:88
  261.8 1.4 copy-start
  361.6 236.5 %all-reduce.12.cloned.1.call-start = ((), (), s32[]{:S(2)}) async-start(), calls=%async_computation.5 | async-start | bytes 1179648 | tf_op jit(solution)/shard_map/psum | solution.py:68
  482.4 333.7 %all-reduce.14.cloned.1.call-start = ((), (), s32[]{:S(2)}) async-start(), calls=%async_computation.6 | async-start | bytes 2359296 | tf_op jit(solution)/shard_map/psum | solution.py:88
  598.1 1.4 copy-start.1
  698.8 236.5 %all-reduce.16.cloned.1.call-start = ((), (), s32[]{:S(2)}) async-start(), calls=%async_computation.7 | async-start | bytes 1179648 | tf_op jit(solution)/shard_map/psum | solution.py:68
  819.6 305.3 %reduce-scatter.4.cloned.1.call-start = ((), (), s32[]{:S(2)}) async-start(), calls=%async_computation.9 | async-start | bytes 1253376
  935.3 1.4 copy-start.2
  1035.7 149.8 %all-gather.8.cloned.1.call-start = ((), (), s32[]{:S(2)}) async-start(), calls=%async_computation.8 | async-start | bytes 1253376 | tf_op jit(solution)/shard_map/all_gather | solution.py:96
  1124.9 62.0 %collective-permute-start = (f32[24,768]{1,0:T(8,128)}, f32[24,768]{1,0:T(8,128)S(1)}, u32[]{:S(2)}, u32[]{:S(2)}) collective-permute-start(f32[24,768]{1,0:T(8,128)} %reduce-scatter.4.cloned.1.call-done), channel_id=1, source_target_pairs={{0,16},{16,32},{32,48},{48,64},{64,80},{80,96},{96,112},{112,128},... | collective-permute-start | bytes 221192 | tf_op jit(solution)/shard_map/ppermute | solution.py:15
Sparse Core Ops, SparseCore 0:
  10.3 62.2 all-gather.3
  74.8 70.3 all-gather.5
  148.8 112.8 all-reduce.7
  361.7 117.1 all-reduce.9
  482.5 115.5 all-reduce.11
  698.9 117.1 all-reduce.13
  819.7 115.5 all-reduce.15
  1035.8 88.9 reduce-scatter.3
  1127.9 57.6 all-gather.7
where the time goes:
time: 1200 us
  waiting for transfers between devices  846 us (70%)
  other arithmetic  259 us (22%)
  matrix products  31.1 us (3%)
  local copies, waits for them, and re-layouts  28.3 us (2%)
  between operations  28.1 us (2%)
    psum x3, waiting for transfers between devices, orthonormal(): gram_matrix = lax.psum(inner_rows(sketched, sketched), 'row')  344 us
    psum x2, waiting for transfers between devices, on_device(): projected = lax.psum(inner_rows(two_site, ortho_basis), 'row')  235 us
    another operation x32, other arithmetic, orthonormal(): chol_factor = jnp.linalg.cholesky(gram_matrix)  171 us
    unnamed x10, waiting for transfers between devices  89.9 us
    another operation x8, other arithmetic, orthonormal(): lax.linalg.triangular_solve(chol_factor, sketched, left_side=False, lower...  88.6 us
    all_gather x1, waiting for transfers between devices, on_device(): shard_part = lax.all_gather(sketch, 'bond', axis=0, tiled=True)  68.8 us
    all_gather x1, waiting for transfers between devices, on_device(): shard_part = lax.all_gather(stacked_final, 'row', axis=0, tiled=True)  59.4 us
    all_gather x1, waiting for transfers between devices, on_device(): shard_part = lax.all_gather(right_core, 'row', axis=1, tiled=True)  49.4 us
  transfers between devices with their start and end apart: 10, of which 9 were waited for; matrix products, arithmetic and copies ran while one was open for 1% of the time, Pallas kernels for 0%

commit v1 on v0

--- a/solution.py
+++ b/solution.py
@@ -77,7 +77,9 @@
     local_sites = left_core.shape[1]
     local_rows = 2 * local_sites
     left_matrix = left_core.reshape(local_rows, width)
-    shard_part = lax.all_gather(right_core, "row", axis=1, tiled=True)
+    shard_part = jnp.concatenate(
+        lax.all_to_all(jnp.stack([right_core] * lax.axis_size("row")), "row", 0, 0), axis=1
+    )
     count = shard_part.shape[1]
     two_site = matmul(left_matrix, shard_part.reshape(count, 2 * width))
     two_site = apply_gate(two_site, build_gate(gate_angles[0]))

time: 1200 us -> 1140 us (0.950)
  waiting for transfers between devices: 846 us -> 780 us
    all_gather x1 -> x0, waiting for transfers between devices: 49.4 us -> none  [on_device(): shard_part = lax.all_gather(right_core, 'row', axis=1, tiled=True)]
    all_gather x1, waiting for transfers between devices: 68.8 us -> 47.1 us  [on_device(): shard_part = lax.all_gather(sketch, 'bond', axis=0, tiled=True)]
    unnamed x10 -> x9, waiting for transfers between devices: 89.9 us -> 89.2 us
where the time goes in v1:
time: 1140 us
  waiting for transfers between devices  780 us (68%)
  other arithmetic  259 us (23%)
  between operations  28.6 us (3%)
  local copies, waits for them, and re-layouts  28.5 us (2%)
  matrix products  26.8 us (2%)
  starting transfers between devices  11.9 us (1%)
    psum x3, waiting for transfers between devices, orthonormal(): gram_matrix = lax.psum(inner_rows(sketched, sketched), 'row')  344 us
    psum x2, waiting for transfers between devices, on_device(): projected = lax.psum(inner_rows(two_site, ortho_basis), 'row')  235 us
    another operation x32, other arithmetic, orthonormal(): chol_factor = jnp.linalg.cholesky(gram_matrix)  171 us
    unnamed x9, waiting for transfers between devices  89.2 us
    another operation x8, other arithmetic, orthonormal(): lax.linalg.triangular_solve(chol_factor, sketched, left_side=False, lower...  88.6 us
    all_gather x1, waiting for transfers between devices, on_device(): shard_part = lax.all_gather(stacked_final, 'row', axis=0, tiled=True)  59.4 us
    all_gather x1, waiting for transfers between devices, on_device(): shard_part = lax.all_gather(sketch, 'bond', axis=0, tiled=True)  47.1 us
  transfers between devices with their start and end apart: 10, of which 9 were waited for; matrix products, arithmetic and copies ran while one was open for 1% of the time, Pallas kernels for 0%

profile of v1, /device:TPU:2, one launch (start us, length us, event | category | flops | bytes accessed | tf_op | source)
XLA Modules:
  0.0 1135.0 jit_solution(15881413571283322217)
XLA Ops:
  6.5 0.7 all-gather.3.cloned.1.call-update
  7.3 2.2 stack.2
  9.6 9.5 all-to-all-start
  19.2 0.7 fusion.124
  29.3 5.7 all-to-all-done
  36.0 0.8 fusion.2
  36.8 0.7 fusion.8
  37.5 47.1 %all-gather.3.cloned.1.call-done = f32[768,384]{1,0:T(8,128)} async-done(((f32[24,384]{1,0:T(8,128)}), f32[768,384]{1,0:T(8,128)}) %all-gather.3.cloned.1.call-update) | async-done | bytes 1179664 | tf_op jit(solution)/shard_map/all_gather | solution.py:86
  84.6 2.0 fusion.125
  86.6 1.5 fusion.126
  88.7 112.6 %all-reduce.8.cloned.1.call-done = f32[384,384]{0,1:T(8,128)} async-done(((f32[384,384]{0,1:T(8,128)}), f32[384,384]{0,1:T(8,128)}) %all-reduce.8.cloned.1.call-update) | async-done | bytes 589840 | tf_op jit(solution)/shard_map/psum | solution.py:68
  201.3 1.4 copy.32
  202.8 11.7 %cholesky.273 = f32[128,128]{1,0:T(8,128)S(1)} custom-call(f32[128,128]{1,0:T(8,128)S(1)} %cholesky.428), custom_call_target="Cholesky" | custom-call | tf_op jit(solution)/shard_map/jit(cholesky)/cholesky | solution.py:69
  214.6 9.8 custom-call.23
  224.9 11.7 %cholesky.292 = f32[128,128]{1,0:T(8,128)S(1)} custom-call(f32[128,128]{1,0:T(8,128)S(1)} %cholesky.432), custom_call_target="Cholesky" | custom-call | tf_op jit(solution)/shard_map/jit(cholesky)/cholesky | solution.py:69
  236.7 9.9 custom-call.24
  247.1 11.7 %cholesky.311 = f32[128,128]{1,0:T(8,128)S(1)} custom-call(f32[128,128]{1,0:T(8,128)S(1)} %convolution_subtract_fusion.5), custom_call_target="Cholesky" | custom-call | tf_op jit(solution)/shard_map/jit(cholesky)/cholesky | solution.py:69
  258.9 0.7 compare_reduce_fusion.6
  262.3 6.1 while.6
  262.9 1.3 bitcast_dynamic-update-slice_fusion.6
  265.0 1.3 bitcast_dynamic-update-slice_fusion.6
  267.0 1.3 bitcast_dynamic-update-slice_fusion.6
  268.4 29.5 %custom-call.25 = f32[3,128,128]{1,2,0:T(8,128)S(1)} custom-call(f32[3,128,128]{2,1,0:T(8,128)S(1)} %get-tuple-element.27), custom_call_target="InvertDiagBlocksLowerTriangular" | custom-call | tf_op jit(solution)/shard_map/triangular_solve/custom-call.2 | solution.py:70
  298.9 2.2 fusion.22
  301.2 117.3 %all-reduce.10.cloned.1.call-done = f32[768,384]{1,0:T(8,128)} async-done(((f32[768,384]{1,0:T(8,128)}), f32[768,384]{1,0:T(8,128)}) %all-reduce.10.cloned.1.call-update) | async-done | bytes 1179664 | tf_op jit(solution)/shard_map/psum | solution.py:90
  418.4 2.0 fusion.127
  420.4 1.5 fusion.128
  422.2 115.5 %all-reduce.12.cloned.1.call-done = f32[384,384]{0,1:T(8,128)} async-done(((f32[384,384]{0,1:T(8,128)}), f32[384,384]{0,1:T(8,128)}) %all-reduce.12.cloned.1.call-update) | async-done | bytes 589840 | tf_op jit(solution)/shard_map/psum | solution.py:68
  537.7 1.4 copy.34
  539.1 11.7 %cholesky.326 = f32[128,128]{1,0:T(8,128)S(1)} custom-call(f32[128,128]{1,0:T(8,128)S(1)} %cholesky.436), custom_call_target="Cholesky" | custom-call | tf_op jit(solution)/shard_map/jit(cholesky)/cholesky | solution.py:69
  550.9 9.8 custom-call.26
  561.3 11.7 %cholesky.345 = f32[128,128]{1,0:T(8,128)S(1)} custom-call(f32[128,128]{1,0:T(8,128)S(1)} %cholesky.440), custom_call_target="Cholesky" | custom-call | tf_op jit(solution)/shard_map/jit(cholesky)/cholesky | solution.py:69
  573.0 10.2 custom-call.27
  583.7 11.7 %cholesky.364 = f32[128,128]{1,0:T(8,128)S(1)} custom-call(f32[128,128]{1,0:T(8,128)S(1)} %convolution_subtract_fusion.4), custom_call_target="Cholesky" | custom-call | tf_op jit(solution)/shard_map/jit(cholesky)/cholesky | solution.py:69
  595.5 0.7 compare_reduce_fusion.5
  599.4 6.1 while.7
  600.1 1.3 bitcast_dynamic-update-slice_fusion.7
  602.2 1.3 bitcast_dynamic-update-slice_fusion.7
  604.2 1.3 bitcast_dynamic-update-slice_fusion.7
  605.6 29.5 %custom-call.28 = f32[3,128,128]{1,2,0:T(8,128)S(1)} custom-call(f32[3,128,128]{2,1,0:T(8,128)S(1)} %get-tuple-element.28), custom_call_target="InvertDiagBlocksLowerTriangular" | custom-call | tf_op jit(solution)/shard_map/triangular_solve/custom-call.2 | solution.py:70
  636.1 2.2 fusion.28
  638.4 117.3 %all-reduce.14.cloned.1.call-done = f32[768,384]{1,0:T(8,128)} async-done(((f32[768,384]{1,0:T(8,128)}), f32[768,384]{1,0:T(8,128)}) %all-reduce.14.cloned.1.call-update) | async-done | bytes 1179664 | tf_op jit(solution)/shard_map/psum | solution.py:90
  755.6 2.0 fusion.129
  757.6 1.5 fusion.130
  759.3 115.5 %all-reduce.16.cloned.1.call-done = f32[384,384]{0,1:T(8,128)} async-done(((f32[384,384]{0,1:T(8,128)}), f32[384,384]{0,1:T(8,128)}) %all-reduce.16.cloned.1.call-update) | async-done | bytes 589840 | tf_op jit(solution)/shard_map/psum | solution.py:68
  874.8 1.4 copy.36
  876.3 11.7 %cholesky.379 = f32[128,128]{1,0:T(8,128)S(1)} custom-call(f32[128,128]{1,0:T(8,128)S(1)} %cholesky.444), custom_call_target="Cholesky" | custom-call | tf_op jit(solution)/shard_map/jit(cholesky)/cholesky | solution.py:69
  888.1 9.8 custom-call.29
  898.5 11.7 %cholesky.398 = f32[128,128]{1,0:T(8,128)S(1)} custom-call(f32[128,128]{1,0:T(8,128)S(1)} %cholesky.448), custom_call_target="Cholesky" | custom-call | tf_op jit(solution)/shard_map/jit(cholesky)/cholesky | solution.py:69
  910.2 10.0 custom-call.30
  920.7 11.7 %cholesky.417 = f32[128,128]{1,0:T(8,128)S(1)} custom-call(f32[128,128]{1,0:T(8,128)S(1)} %convolution_subtract_fusion.3), custom_call_target="Cholesky" | custom-call | tf_op jit(solution)/shard_map/jit(cholesky)/cholesky | solution.py:69
  932.5 0.7 compare_reduce_fusion.2
  936.4 6.1 while.8
  937.1 1.3 bitcast_dynamic-update-slice_fusion.8
  939.2 1.3 bitcast_dynamic-update-slice_fusion.8
  941.2 1.3 bitcast_dynamic-update-slice_fusion.8
  942.6 29.5 %custom-call.31 = f32[3,128,128]{1,2,0:T(8,128)S(1)} custom-call(f32[3,128,128]{2,1,0:T(8,128)S(1)} %get-tuple-element.29), custom_call_target="InvertDiagBlocksLowerTriangular" | custom-call | tf_op jit(solution)/shard_map/triangular_solve/custom-call.2 | solution.py:70
  973.1 2.1 fusion.120
  975.3 0.7 reshape.76
  976.0 88.4 %reduce-scatter.4.cloned.1.call-done = f32[24,768]{1,0:T(8,128)} async-done(((f32[384,768]{1,0:T(8,128)}), f32[24,768]{1,0:T(8,128)}) %reduce-scatter.4.cloned.1.call-update) | async-done | bytes 73744
  1064.4 1.3 collective-permute-start
  1065.7 59.4 %all-gather.5.cloned.1.call-done = f32[384,2,384]{2,1,0:T(2,128)} async-done(((f32[24,2,384]{2,1,0:T(2,128)}), f32[384,2,384]{2,1,0:T(2,128)}) %all-gather.5.cloned.1.call-update) | async-done | bytes 1179664 | tf_op jit(solution)/shard_map/all_gather | solution.py:98
  1125.1 1.3 copy.49
  1126.5 1.5 convolution_bitcast_fusion
  (141 shorter events, 19.4 us)
Async XLA Ops:
  6.5 78.1 %all-gather.3.cloned.1.call-start = ((), (), s32[]{:S(2)}) async-start(), calls=%async_computation.2 | async-start | bytes 1216512 | tf_op jit(solution)/shard_map/all_gather | solution.py:86
  9.5 9.7 copy-start.4
  9.5 18.8 %copy-start.9 = (f32[4,4]{1,0:T(4,128)S(1)}, f32[4,4]{1,0:T(4,128)}, u32[]{:S(2)}) copy-start(f32[4,4]{1,0:T(4,128)} %constant.102.clone) | copy-start | bytes 196
  9.5 18.8 %copy-start.10 = (f32[4,4]{1,0:T(4,128)S(1)}, f32[4,4]{1,0:T(4,128)}, u32[]{:S(2)}) copy-start(f32[4,4]{1,0:T(4,128)} %constant.103.clone) | copy-start | bytes 196
  9.5 18.8 %copy-start.16 = (f32[4,4]{1,0:T(4,128)S(1)}, f32[4,4]{1,0:T(4,128)}, u32[]{:S(2)}) copy-start(f32[4,4]{1,0:T(4,128)} %constant.104.clone) | copy-start | bytes 196
  9.5 18.9 %copy-start.15 = (f32[4,4]{1,0:T(4,128)S(1)}, f32[4,4]{1,0:T(4,128)}, u32[]{:S(2)}) copy-start(f32[4,4]{1,0:T(4,128)} %constant.105.clone) | copy-start | bytes 196
  9.5 19.1 %copy-start.7 = (f32[4,4]{1,0:T(4,128)S(1)}, f32[4,4]{1,0:T(4,128)}, u32[]{:S(2)}) copy-start(f32[4,4]{1,0:T(4,128)} %constant.106.clone) | copy-start | bytes 196
  9.5 19.1 %copy-start.8 = (f32[4,4]{1,0:T(4,128)S(1)}, f32[4,4]{1,0:T(4,128)}, u32[]{:S(2)}) copy-start(f32[4,4]{1,0:T(4,128)} %constant.107.clone) | copy-start | bytes 196
  9.5 19.1 %copy-start.14 = (f32[4,4]{1,0:T(4,128)S(1)}, f32[4,4]{1,0:T(4,128)}, u32[]{:S(2)}) copy-start(f32[4,4]{1,0:T(4,128)} %constant.108.clone) | copy-start | bytes 196
  9.6 19.2 %copy-start.13 = (f32[4,4]{1,0:T(4,128)S(1)}, f32[4,4]{1,0:T(4,128)}, u32[]{:S(2)}) copy-start(f32[4,4]{1,0:T(4,128)} %constant.109.clone) | copy-start | bytes 196
  9.6 19.3 %copy-start.5 = (f32[4,4]{1,0:T(4,128)S(1)}, f32[4,4]{1,0:T(4,128)}, u32[]{:S(2)}) copy-start(f32[4,4]{1,0:T(4,128)} %constant.110.clone) | copy-start | bytes 196
  9.6 19.3 %copy-start.6 = (f32[4,4]{1,0:T(4,128)S(1)}, f32[4,4]{1,0:T(4,128)}, u32[]{:S(2)}) copy-start(f32[4,4]{1,0:T(4,128)} %constant.111.clone) | copy-start | bytes 196
  9.6 19.3 %copy-start.12 = (f32[4,4]{1,0:T(4,128)S(1)}, f32[4,4]{1,0:T(4,128)}, u32[]{:S(2)}) copy-start(f32[4,4]{1,0:T(4,128)} %constant.112.clone) | copy-start | bytes 196
  9.6 19.4 %copy-start.11 = (f32[4,4]{1,0:T(4,128)S(1)}, f32[4,4]{1,0:T(4,128)}, u32[]{:S(2)}) copy-start(f32[4,4]{1,0:T(4,128)} %constant.113.clone) | copy-start | bytes 196
  9.6 25.4 %all-to-all-start = ((f32[16,1,24,2,384]{4,3,2,1,0:T(2,128)}), f32[16,1,24,2,384]{4,3,2,1,0:T(2,128)S(1)}, u32[]{:S(2)}, u32[]{:S(2)}) async-start(f32[16,1,24,2,384]{4,3,2,1,0:T(2,128)} %stack.2), calls=%async_computation | async-start | bytes 2359296 | tf_op jit(solution)/shard_map/all_to_all | solution.py:81
  19.1 182.2 %all-reduce.8.cloned.1.call-start = ((), (), s32[]{:S(2)}) async-start(), calls=%async_computation.3 | async-start | bytes 1179648 | tf_op jit(solution)/shard_map/psum | solution.py:68
  35.1 0.9 copy-start.3
  88.1 330.3 %all-reduce.10.cloned.1.call-start = ((), (), s32[]{:S(2)}) async-start(), calls=%async_computation.4 | async-start | bytes 2359296 | tf_op jit(solution)/shard_map/psum | solution.py:90
  201.3 1.4 copy-start
  301.1 236.5 %all-reduce.12.cloned.1.call-start = ((), (), s32[]{:S(2)}) async-start(), calls=%async_computation.5 | async-start | bytes 1179648 | tf_op jit(solution)/shard_map/psum | solution.py:68
  421.9 333.7 %all-reduce.14.cloned.1.call-start = ((), (), s32[]{:S(2)}) async-start(), calls=%async_computation.6 | async-start | bytes 2359296 | tf_op jit(solution)/shard_map/psum | solution.py:90
  537.7 1.4 copy-start.1
  638.3 236.5 %all-reduce.16.cloned.1.call-start = ((), (), s32[]{:S(2)}) async-start(), calls=%async_computation.7 | async-start | bytes 1179648 | tf_op jit(solution)/shard_map/psum | solution.py:68
  759.1 305.3 %reduce-scatter.4.cloned.1.call-start = ((), (), s32[]{:S(2)}) async-start(), calls=%async_computation.9 | async-start | bytes 1253376
  874.8 1.4 copy-start.2
  975.3 149.8 %all-gather.5.cloned.1.call-start = ((), (), s32[]{:S(2)}) async-start(), calls=%async_computation.8 | async-start | bytes 1253376 | tf_op jit(solution)/shard_map/all_gather | solution.py:98
  1064.4 62.0 %collective-permute-start = (f32[24,768]{1,0:T(8,128)}, f32[24,768]{1,0:T(8,128)S(1)}, u32[]{:S(2)}, u32[]{:S(2)}) collective-permute-start(f32[24,768]{1,0:T(8,128)} %reduce-scatter.4.cloned.1.call-done), channel_id=1, source_target_pairs={{0,16},{16,32},{32,48},{48,64},{64,80},{80,96},{96,112},{112,128},... | collective-permute-start | bytes 221192 | tf_op jit(solution)/shard_map/ppermute | solution.py:15
Sparse Core Ops, SparseCore 0:
  9.5 75.1 all-gather.2
  88.2 113.0 all-reduce.7
  301.2 117.1 all-reduce.9
  422.0 115.5 all-reduce.11
  638.4 117.1 all-reduce.13
  759.2 115.5 all-reduce.15
  975.4 88.9 reduce-scatter.3
  1067.4 57.6 all-gather.4
